TPU v7x, 32 devices: a whole 2x2x4 slice. The times are simulated.
32 devices in a mesh: cell: 16 (over z, y, core), bin: 2 (over x).
Axes of the slice: x: 2, y: 2, z: 4, core: 2. Of those that a mesh axis runs over, the one named last changes fastest.
Arguments:
- tensor: float32 [96, 4096, 1024], P('cell', None, 'bin'), may hold values from -6 to 6
- cell_factor: float32 [4096, 128], P('cell'), may hold values from -4 to 4
- bin_factor: float32 [1024, 128], P('bin'), may hold values from -4 to 4
Outputs:
- updated: float32 [96, 128], P('cell', 'bin')
All inputs are finite; a program needn't handle non-finite values.
Results may differ from a plain program's by a relative error of at most 0.000096.
Values sent between devices are 32-bit elements; how exact they have to be, the bound alone decides.
No kernel may reach another device: no remote copies, remote signals or barrier semaphores. Data moves between devices by JAX's collectives and lax.ppermute only.
A program may use at most 128 MiB of HBM per device.

v0:
```python
import jax
import jax.numpy as jnp
from jax import lax
from jax.sharding import PartitionSpec as P


def body(tensor, cell_factor, bin_factor):
    highest = lax.Precision.HIGHEST
    image_rows, cell_count, bin_count = tensor.shape
    rank_cols = bin_factor.shape[1]
    projected = jnp.dot(
        tensor.reshape(image_rows * cell_count, bin_count), bin_factor, precision=highest
    )
    projected = projected.reshape(image_rows, cell_count, rank_cols)
    bin_local = jnp.dot(bin_factor.T, bin_factor, precision=highest)
    gram_bin = lax.psum(bin_local, "bin")
    mttkrp = jnp.sum(
        projected * lax.all_gather(cell_factor, "cell", axis=0, tiled=True)[None, :, :], axis=1
    )
    cell_local = jnp.dot(cell_factor.T, cell_factor, precision=highest)
    gram_cell = lax.psum(cell_local, "cell")
    gram = gram_cell * gram_bin
    chol_lower = jnp.linalg.cholesky(gram)
    totals = lax.psum(mttkrp, "bin")
    solved = jax.scipy.linalg.cho_solve((chol_lower, True), totals.T).T
    own_cols = rank_cols // lax.axis_size("bin")
    updated = lax.dynamic_slice_in_dim(solved, lax.axis_index("bin") * own_cols, own_cols, 1)
    return updated


def solution(mesh):
    placed = (P("cell", None, "bin"), P("cell", None), P("bin", None))
    return jax.shard_map(
        body, mesh=mesh, in_specs=placed, out_specs=P("cell", "bin"), check_vma=False
    )
```

profile of v0, /device:TPU:0, one launch (start us, length us, event | category | flops | bytes accessed | tf_op | source)
XLA Modules:
  0.0 223.3 jit_solution(393272512199881900)
XLA Ops:
  6.5 0.0 copy-start
  6.5 0.0 all-reduce.3.cloned.1.call-start
  6.5 2.0 fusion.7
  8.6 0.0 all-reduce.3.cloned.1.call-update
  8.6 0.0 all-reduce.5.cloned.1.call-start
  8.6 0.0 copy-done
  8.6 1.2 fusion.8
  9.8 0.0 all-reduce.5.cloned.1.call-update
  9.9 0.0 all-gather.2.cloned.1.call-start
  9.9 0.7 all-gather.2.cloned.1.call-update
  10.6 87.4 %all-reduce.3.cloned.1.call-done = f32[128,128]{0,1:T(8,128)} async-done(((f32[128,128]{0,1:T(8,128)}), f32[128,128]{0,1:T(8,128)}) %all-reduce.3.cloned.1.call-update) | async-done | bytes 65552 | tf_op jit(solution)/shard_map/psum | solution.py:21
  98.0 24.7 %all-reduce.5.cloned.1.call-done = f32[128,128]{0,1:T(8,128)} async-done(((f32[128,128]{0,1:T(8,128)}), f32[128,128]{0,1:T(8,128)}) %all-reduce.5.cloned.1.call-update) | async-done | bytes 65552 | tf_op jit(solution)/shard_map/psum | solution.py:16
  122.7 0.9 mul.14
  123.6 0.1 copy.9
  123.7 11.7 %cholesky.16 = f32[128,128]{1,0:T(8,128)S(1)} custom-call(f32[128,128]{1,0:T(8,128)S(1)} %fusion.6), custom_call_target="Cholesky" | custom-call | tf_op jit(solution)/shard_map/jit(cholesky)/cholesky | solution.py:23
  135.5 0.6 compare_reduce_fusion
  136.1 0.7 fusion.1
  136.8 9.8 %custom-call.10 = f32[1,128,128]{1,2,0:T(8,128)S(1)} custom-call(f32[1,128,128]{2,1,0:T(8,128)S(1)} %fusion.1), custom_call_target="InvertDiagBlocksLowerTriangular" | custom-call | tf_op jit(solution)/shard_map/jit(_cho_solve)/triangular_solve | solution.py:25
  146.6 20.2 %all-gather.2.cloned.1.call-done = f32[4096,128]{1,0:T(8,128)} async-done(((f32[256,128]{1,0:T(8,128)}), f32[4096,128]{1,0:T(8,128)}) %all-gather.2.cloned.1.call-update) | async-done | bytes 2097168 | tf_op jit(solution)/shard_map/all_gather | solution.py:18
  166.8 43.8 %multiply_reduce_fusion = f32[6,128]{1,0:T(8,128)S(1)} fusion(f32[6,4096,512]{2,1,0:T(8,128)} %param.3, f32[4096,128]{1,0:T(8,128)} %all-gather.2.cloned.1.call-done, f32[512,128]{1,0:T(8,128)S(1)} %copy-done), kind=kOutput, calls=%fused_computation | convolution fusion | flops 19333644288 | bytes 52694016 | tf_op jit(solution)/shard_map/dot_general | solution.py:11
  210.7 4.9 %psum.23 = f32[6,128]{1,0:T(8,128)S(1)} all-reduce(f32[6,128]{1,0:T(8,128)S(1)} %multiply_reduce_fusion), channel_id=1, replica_groups=mesh['cell'=16,'bin'=2] {'bin'}, use_global_device_ids=true, to_apply=%region_5.6 | all-reduce | flops 768 | bytes 6144 | tf_op jit(solution)/shard_map/psum | solution.py:24
  215.6 0.3 fusion.4
  215.9 0.2 fusion.2
  216.1 0.7 constant_dynamic-slice_fusion
  (2 shorter events, 0.0 us)
Async XLA Ops:
  6.5 2.1 copy-start
  6.5 91.5 %all-reduce.3.cloned.1.call-start = ((), (), s32[]{:S(2)}) async-start(), calls=%async_computation | async-start | bytes 131072 | tf_op jit(solution)/shard_map/psum | solution.py:21
  8.6 114.1 %all-reduce.5.cloned.1.call-start = ((), (), s32[]{:S(2)}) async-start(), calls=%async_computation.1 | async-start | bytes 131072 | tf_op jit(solution)/shard_map/psum | solution.py:16
  9.9 156.9 %all-gather.2.cloned.1.call-start = ((), (), s32[]{:S(2)}) async-start(), calls=%async_computation.2 | async-start | bytes 2228224 | tf_op jit(solution)/shard_map/all_gather | solution.py:18
Sparse Core Ops, SparseCore 0:
  10.8 87.1 all-reduce.2
  100.3 22.3 all-reduce.4
  125.1 41.6 all-gather.1
where the time goes:
time: 224 us; the launch traced here: 223 us
  waiting for transfers between devices  133 us (59%)
  matrix products  47.5 us (21%)
  other arithmetic  23.8 us (11%)
  between operations  13.2 us (6%)
  blocking collectives  4.95 us (2%)
    psum x1, waiting for transfers between devices, body(): gram_cell = lax.psum(cell_local, 'cell')  87.4 us
    dot_general x1, matrix products, body(): jnp.dot(tensor.reshape(image_rows * cell_count, bin_count), bin_factor, p...  43.8 us
    psum x1, waiting for transfers between devices, body(): gram_bin = lax.psum(bin_local, 'bin')  24.7 us
    all_gather x1, waiting for transfers between devices, body(): lax.all_gather(cell_factor, 'cell', axis=0, tiled=True)[None, :, :]  20.2 us
    another operation x3, other arithmetic, body(): chol_lower = jnp.linalg.cholesky(gram)  12.4 us
    another operation x2, other arithmetic, body(): solved = jax.scipy.linalg.cho_solve((chol_lower, True), totals.T).T  10.5 us
    psum x1, blocking collectives, body(): totals = lax.psum(mttkrp, 'bin')  4.95 us
  transfers between devices with their start and end apart: 3, of which 3 were waited for; matrix products, arithmetic and copies ran while one was open for 11% of the time, Pallas kernels for 0%

commit v1 on v0

--- a/solution.py
+++ b/solution.py
@@ -13,7 +13,7 @@
     )
     projected = projected.reshape(image_rows, cell_count, rank_cols)
     bin_local = jnp.dot(bin_factor.T, bin_factor, precision=highest)
-    gram_bin = lax.psum(bin_local, "bin")
+    gram_bin = jnp.sum(jax.lax.all_gather(bin_local, axis_name="bin"), 0)
     mttkrp = jnp.sum(
         projected * lax.all_gather(cell_factor, "cell", axis=0, tiled=True)[None, :, :], axis=1
     )

time: 224 us -> 200 us (0.89)
  waiting for transfers between devices: 133 us -> 105 us
  blocking collectives: 4.95 us -> 10.8 us
    psum x1 -> x0, waiting for transfers between devices: 24.7 us -> none  [body(): gram_bin = lax.psum(bin_local, 'bin')]
    all_gather x0 -> x1, blocking collectives: none -> 5.84 us  [body(): gram_bin = jnp.sum(jax.lax.all_gather(bin_local, axis_name='bin'), 0)]
    psum x1, waiting for transfers between devices: 87.4 us -> 82.1 us  [body(): gram_cell = lax.psum(cell_local, 'cell')]
  transfers between devices with their start and end apart: 3 -> 2, of which waited for: 3 -> 2; matrix products, arithmetic and copies ran while one was open for 11% -> 12% of each run, Pallas kernels for 0% -> 0%
where the time goes in v1:
time: 200 us
  waiting for transfers between devices  105 us (52%)
  matrix products  46.8 us (23%)
  other arithmetic  23.7 us (12%)
  between operations  13.5 us (7%)
  blocking collectives  10.8 us (5%)
    psum x1, waiting for transfers between devices, body(): gram_cell = lax.psum(cell_local, 'cell')  82.1 us
    dot_general x1, matrix products, body(): jnp.dot(tensor.reshape(image_rows * cell_count, bin_count), bin_factor, p...  43.8 us
    all_gather x1, waiting for transfers between devices, body(): lax.all_gather(cell_factor, 'cell', axis=0, tiled=True)[None, :, :]  21.7 us
    another operation x3, other arithmetic, body(): chol_lower = jnp.linalg.cholesky(gram)  12.4 us
    another operation x2, other arithmetic, body(): solved = jax.scipy.linalg.cho_solve((chol_lower, True), totals.T).T  10.5 us
    all_gather x1, blocking collectives, body(): gram_bin = jnp.sum(jax.lax.all_gather(bin_local, axis_name='bin'), 0)  5.84 us
    psum x1, blocking collectives, body(): totals = lax.psum(mttkrp, 'bin')  4.95 us
  transfers between devices with their start and end apart: 2, of which 2 were waited for; matrix products, arithmetic and copies ran while one was open for 12% of the time, Pallas kernels for 0%

profile of v1, /device:TPU:0, one launch (start us, length us, event | category | flops | bytes accessed | tf_op | source)
XLA Modules:
  0.0 200.2 jit_solution(12888665714596438592)
XLA Ops:
  6.5 0.0 copy-start
  6.5 0.0 all-reduce.2.cloned.1.call-start
  6.5 2.0 %fusion.7 = f32[128,128]{0,1:T(8,128)} fusion(f32[256,128]{1,0:T(8,128)} %param.4), kind=kOutput, calls=%fused_computation.15 | convolution fusion | flops 50331648 | bytes 196608 | tf_op jit(solution)/shard_map/dot_general | solution.py:20
  8.6 0.0 all-reduce.2.cloned.1.call-update
  8.6 0.0 all-gather.3.cloned.1.call-start
  8.6 0.7 all-gather.3.cloned.1.call-update
  9.3 0.0 copy-done
  9.3 0.6 fusion.8
  9.9 5.8 %all-gather = f32[256,128]{1,0:T(8,128)S(1)} all-gather(f32[128,128]{1,0:T(8,128)S(1)} %fusion.8), channel_id=2, replica_groups=mesh['cell'=16,'bin'=2] {'bin'}, dimensions={0}, use_global_device_ids=true | all-gather | bytes 196608 | tf_op jit(solution)/shard_map/all_gather | solution.py:16
  15.8 0.1 copy.10
  15.9 82.1 %all-reduce.2.cloned.1.call-done = f32[128,128]{0,1:T(8,128)} async-done(((f32[128,128]{0,1:T(8,128)}), f32[128,128]{0,1:T(8,128)}) %all-reduce.2.cloned.1.call-update) | async-done | bytes 65552 | tf_op jit(solution)/shard_map/psum | solution.py:21
  98.0 0.8 mul.14
  98.9 0.1 copy.11
  99.0 11.7 %cholesky.16 = f32[128,128]{1,0:T(8,128)S(1)} custom-call(f32[128,128]{1,0:T(8,128)S(1)} %fusion.6), custom_call_target="Cholesky" | custom-call | tf_op jit(solution)/shard_map/jit(cholesky)/cholesky | solution.py:23
  110.7 0.6 compare_reduce_fusion
  111.4 0.7 fusion.1
  112.0 9.8 %custom-call.10 = f32[1,128,128]{1,2,0:T(8,128)S(1)} custom-call(f32[1,128,128]{2,1,0:T(8,128)S(1)} %fusion.1), custom_call_target="InvertDiagBlocksLowerTriangular" | custom-call | tf_op jit(solution)/shard_map/jit(_cho_solve)/triangular_solve | solution.py:25
  121.8 21.7 %all-gather.3.cloned.1.call-done = f32[4096,128]{1,0:T(8,128)} async-done(((f32[256,128]{1,0:T(8,128)}), f32[4096,128]{1,0:T(8,128)}) %all-gather.3.cloned.1.call-update) | async-done | bytes 2097168 | tf_op jit(solution)/shard_map/all_gather | solution.py:18
  143.5 43.8 %multiply_reduce_fusion = f32[6,128]{1,0:T(8,128)S(1)} fusion(f32[6,4096,512]{2,1,0:T(8,128)} %param.3, f32[4096,128]{1,0:T(8,128)} %all-gather.3.cloned.1.call-done, f32[512,128]{1,0:T(8,128)S(1)} %copy-done), kind=kOutput, calls=%fused_computation | convolution fusion | flops 19333644288 | bytes 52694016 | tf_op jit(solution)/shard_map/dot_general | solution.py:11
  187.4 4.9 %psum.15 = f32[6,128]{1,0:T(8,128)S(1)} all-reduce(f32[6,128]{1,0:T(8,128)S(1)} %multiply_reduce_fusion), channel_id=1, replica_groups=mesh['cell'=16,'bin'=2] {'bin'}, use_global_device_ids=true, to_apply=%region_5.6 | all-reduce | flops 768 | bytes 6144 | tf_op jit(solution)/shard_map/psum | solution.py:24
  192.3 0.2 fusion.4
  192.5 0.2 fusion.2
  192.7 0.7 constant_dynamic-slice_fusion
  (3 shorter events, 0.1 us)
Async XLA Ops:
  6.5 2.8 %copy-start = (f32[512,128]{1,0:T(8,128)S(1)}, f32[512,128]{1,0:T(8,128)}, u32[]{:S(2)}) copy-start(f32[512,128]{1,0:T(8,128)} %param.5) | copy-start | bytes 786436
  6.5 91.5 %all-reduce.2.cloned.1.call-start = ((), (), s32[]{:S(2)}) async-start(), calls=%async_computation | async-start | bytes 131072 | tf_op jit(solution)/shard_map/psum | solution.py:21
  8.6 135.0 %all-gather.3.cloned.1.call-start = ((), (), s32[]{:S(2)}) async-start(), calls=%async_computation.1 | async-start | bytes 2228224 | tf_op jit(solution)/shard_map/all_gather | solution.py:18
Sparse Core Ops, SparseCore 0:
  10.8 87.1 all-reduce.1
  100.4 43.0 all-gather.2
